TPU v7x, 256 devices: a whole 4x4x8 slice. The times are simulated.
256 devices in a mesh: tm: 64 (over z, x_hi, y), chan: 4 (over x_lo, core).
Axes of the slice: x: 4 (x_hi: 2, x_lo: 2; x = x_hi * 2 + x_lo), y: 4, z: 8, core: 2. Of those that a mesh axis runs over, the one named last changes fastest.
Arguments:
- signal: float32 [256, 8192], P('chan', 'tm'), may hold values from -256 to 256
- support: int32 [32], replicated, may hold values from 1 to 4, as said below
- pair_first: int32 [4, 512], replicated, may hold values from 0 to 255
- pair_second: int32 [4, 512], replicated, may hold values from 0 to 255
- pair_count: int32 [4], replicated, may hold values from 128 to 512, as said below
Outputs:
- cross: float32 [4, 512, 2, 32], P('chan', 'tm')
- coherence: float32 [4, 512, 32], P('chan', 'tm')
Inputs may be any that keep to these rules, and one draw needn't show every extreme that they name: With b = q // 8 the band of scale q, support[q] is at most (4 * 128 / 4^(3 - b) + 127) // 128, and equals it for the last scale of every band. The live slots of an owner are its first pair_count slots; some owner has all 512 slots live.
All inputs are finite; a program needn't handle non-finite values.
Results may differ from a plain program's by a relative error of at most 0.0027.
Values may be sent and summed in bfloat16 or wider, within the bound.
No kernel may reach another device: no remote copies, remote signals or barrier semaphores. Data moves between devices by JAX's collectives and lax.ppermute only.
A program may use at most 192 MiB of HBM per device.

v0:
```python
import math
import jax
import jax.numpy as jnp
import numpy as np
from jax import lax
from jax.sharding import PartitionSpec as P

NS = 32
BLK = 128
TD = 128
power_floor = 1e-06


def from_behind(array, axis, by):
    peers = lax.axis_size(axis)
    return lax.ppermute(array, axis, [(i, (i + by) % peers) for i in range(peers)])


def kernel_table(scale_ids, reaches, offsets):
    taps = (2 * offsets + 1) * BLK
    lag = jnp.arange(taps, dtype=jnp.int32) - offsets * BLK
    within = jnp.arange(BLK, dtype=jnp.int32)
    scale_width = 2.0 * TD * jnp.exp2((scale_ids - (NS - 1)).astype(jnp.float32) / 4.0)
    width = scale_width[:, None, None]
    offset = lag[None, :, None] - within[None, None, :]
    scaled_offset = offset.astype(jnp.float32) / width
    amplitude = (
        math.pi ** (-0.25) * lax.rsqrt(width) * jnp.exp(-0.5 * scaled_offset * scaled_offset)
    )
    inside = jnp.abs(offset) < (reaches * BLK)[:, None, None]
    lag_phase = 6.0 * (lag.astype(jnp.float32)[None, :] / scale_width[:, None])
    time_phase = 6.0 * (within.astype(jnp.float32)[None, :] / scale_width[:, None])
    lag_cos = jnp.cos(lag_phase)[:, :, None]
    lag_sin = jnp.sin(lag_phase)[:, :, None]
    time_cos = jnp.cos(time_phase)[:, None, :]
    time_sin = jnp.sin(time_phase)[:, None, :]
    cos_part = lag_cos * time_cos + lag_sin * time_sin
    sin_part = lag_sin * time_cos - lag_cos * time_sin
    real_part = jnp.where(inside, amplitude * cos_part, 0.0).astype(jnp.bfloat16)
    imag_part = jnp.where(inside, amplitude * sin_part, 0.0).astype(jnp.bfloat16)
    return jnp.stack([real_part, imag_part], axis=1)


def band_coefficients(extended, scale_ids, reaches, offsets):
    channels = extended.shape[0]
    table = kernel_table(scale_ids, reaches, offsets)
    coefficients = jnp.einsum("cm,qrmt->qrct", extended, table, preferred_element_type=jnp.float32)
    scale_count = scale_ids.shape[0]
    return coefficients.astype(jnp.bfloat16).reshape(scale_count, 2 * channels, BLK)


def pair_sums(coefficients, first_flat, second_flat):
    scale_count = coefficients.shape[0]
    channels = coefficients.shape[1] // 2
    time_span = coefficients.shape[2]
    chan_iota = jnp.arange(channels, dtype=jnp.int32)
    both = jnp.concatenate([first_flat, second_flat])
    pick = (both[:, None] == chan_iota[None, :]).astype(jnp.bfloat16)
    parts = coefficients.reshape(scale_count, 2, channels, time_span)
    picked = jnp.einsum("pc,qrct->qrpt", pick, parts, preferred_element_type=jnp.bfloat16)
    pairs = first_flat.shape[0]
    first_real = picked[:, 0, :pairs]
    first_imag = picked[:, 1, :pairs]
    second_real = picked[:, 0, pairs:]
    second_imag = picked[:, 1, pairs:]

    def time_sum(left, right):
        return jnp.einsum("qpt,qpt->qp", left, right, preferred_element_type=jnp.float32)

    cross_real = time_sum(first_real, second_real) + time_sum(first_imag, second_imag)
    cross_imag = time_sum(first_imag, second_real) - time_sum(first_real, second_imag)
    power = jnp.einsum("qrct,qrct->qc", parts, parts, preferred_element_type=jnp.float32)
    high = lax.reduce_precision(power, exponent_bits=8, mantissa_bits=7)
    rest = power - high
    middle = lax.reduce_precision(rest, exponent_bits=8, mantissa_bits=7)
    low = rest - middle
    pieces = jnp.stack([high, middle, low]).astype(jnp.bfloat16)
    picked_power = jnp.einsum("pc,kqc->kqp", pick, pieces, preferred_element_type=jnp.float32)
    owner_power = picked_power[0] + picked_power[1] + picked_power[2]
    power_first = owner_power[:, :pairs]
    power_second = owner_power[:, pairs:]
    return jnp.stack([cross_real, cross_imag, power_first, power_second], axis=1)


def shards(signal, support, pair_first, pair_second, pair_count):
    groups = lax.axis_size("chan")
    cluster_number = lax.axis_index("chan")
    time_index = lax.axis_index("tm")
    time_devices = lax.axis_size("tm")
    time_span = signal.shape[1]
    ntime = time_span * time_devices
    rounded = signal.astype(jnp.bfloat16)
    gathered = lax.all_gather(rounded, "chan", axis=0, tiled=True)
    near = jnp.concatenate(
        [from_behind(gathered, "tm", 1), gathered, from_behind(gathered, "tm", -1)], axis=1
    )
    wide = jnp.concatenate([from_behind(near, "tm", 3), near, from_behind(near, "tm", -3)], axis=1)
    per_group = NS // groups
    band = NS // 4
    narrow_count = (NS - band) // groups
    wide_count = band // groups
    narrow_ids = cluster_number * narrow_count + jnp.arange(narrow_count, dtype=jnp.int32)
    wide_ids = NS - band + cluster_number * wide_count + jnp.arange(wide_count, dtype=jnp.int32)
    narrow_coefficients = band_coefficients(near, narrow_ids, support[narrow_ids], 1)
    wide_coefficients = band_coefficients(wide, wide_ids, support[wide_ids], 4)
    owner_devices, slots_total = pair_first.shape
    slots_local = slots_total // time_devices

    def by_block(pairs):
        return (
            pairs.reshape(owner_devices, time_devices, slots_local).transpose(2, 1, 0).reshape(-1)
        )

    first_flat = by_block(pair_first)
    second_flat = by_block(pair_second)
    sums = jnp.concatenate(
        [
            pair_sums(narrow_coefficients, first_flat, second_flat),
            pair_sums(wide_coefficients, first_flat, second_flat),
        ],
        axis=0,
    )
    values = sums.shape[1]
    destinations = time_devices * groups
    partial_value = sums.reshape(per_group * values * slots_local, destinations).T
    partial_value = partial_value.reshape(destinations, 2, -1)
    exchanged = lax.all_to_all(partial_value, ("tm", "chan"), 0, 0, tiled=True)
    summed = jnp.sum(exchanged.reshape(time_devices, groups, -1), axis=0)
    owned = summed.reshape(groups, per_group, values, slots_local) / ntime
    owned = owned.reshape(groups, per_group, values, slots_local)
    owned = jnp.concatenate(
        [
            owned[:, :narrow_count].reshape(groups * narrow_count, values, slots_local),
            owned[:, narrow_count:].reshape(groups * wide_count, values, slots_local),
        ],
        axis=0,
    )
    slot_index = time_index * slots_local + jnp.arange(slots_local, dtype=jnp.int32)
    alive_mask = slot_index < pair_count[cluster_number]
    cross_real = owned[:, 0, :].T
    cross_imag = owned[:, 1, :].T
    first_power = owned[:, 2, :].T
    second_power = owned[:, 3, :].T
    coherence = (cross_real * cross_real + cross_imag * cross_imag) / (
        (first_power + power_floor) * (second_power + power_floor)
    )
    coherence = jnp.where(alive_mask[:, None], coherence, 0.0)[None]
    cross = jnp.stack([cross_real, cross_imag], axis=1)
    cross = jnp.where(alive_mask[:, None, None], cross, 0.0)[None]
    return (cross, coherence.astype(jnp.float32))


def solution(mesh):
    in_specs = (P("chan", "tm"), P(), P(), P(), P())
    out_specs = (P("chan", "tm", None, None), P("chan", "tm", None))
    return jax.shard_map(shards, mesh=mesh, in_specs=in_specs, out_specs=out_specs, check_vma=False)
```

profile of v0, /device:TPU:1, one launch (start us, length us, event | category | flops | bytes accessed | tf_op | source)
XLA Modules:
  0.0 72.6 jit_solution(3698254476402934474)
XLA Ops:
  0.7 0.8 %convert_element_type.133 = bf16[64,128]{1,0:T(8,128)(2,1)S(1)} convert(f32[64,128]{1,0:T(8,128)} %param.5) | non-fusion elementwise | flops 8192 | bytes 49152 | tf_op jit(solution)/shard_map/convert_element_type | solution.py:92
  1.4 8.3 %all_gather.3 = bf16[256,128]{1,0:T(8,128)(2,1)S(1)} all-gather(bf16[64,128]{1,0:T(8,128)(2,1)S(1)} %convert_element_type.133), channel_id=1, replica_groups=mesh['tm'=64,'chan'=4] {'chan'}, dimensions={0}, use_global_device_ids=true | all-gather | bytes 81920 | tf_op jit(solution)/shard_map/all_gather | solution.py:93
  9.7 8.8 %collective-permute-start.1 = (bf16[256,128]{1,0:T(8,128)(2,1)S(1)}, bf16[256,128]{1,0:T(8,128)(2,1)S(1)}, u32[]{:S(2)}, u32[]{:S(2)}) collective-permute-start(bf16[256,128]{1,0:T(8,128)(2,1)S(1)} %all_gather.3), channel_id=1, source_target_pairs={{0,252},{4,0},{8,4},{12,8},{16,12},{20,16},{24,20},{28,24},{32,28}... | collective-permute-start | bytes 196616 | tf_op jit(solution)/shard_map/ppermute | solution.py:16
  18.6 0.6 gather_fusion.1
  19.3 0.6 gather_fusion
  22.3 0.8 %fusion.25 = (bf16[6,1,384,128]{2,3,1,0:T(8,128)(2,1)S(1)}, bf16[6,1,384,128]{2,3,1,0:T(8,128)(2,1)S(1)}) fusion(f32[6,128]{1,0:T(8,128)S(1)} %get-tuple-element.43, f32[6,384]{1,0:T(8,128)S(1)} %get-tuple-element.36, f32[6,128]{1,0:T(8,128)S(1)} %get-tuple-element.42, f32[6,384]{1,0:T(8,128)S(1)} %get-tuple-element.35, f32[6]{0:T(128)S(1)} %get-tuple-element.55, ...), kind=kLoop, calls=%fused_computation.47 | loop fusion | flops 5013504 | bytes 1597512 | tf_op jit(solution)/shard_map/convert_element_type | solution.py:39
  23.1 1.0 %fusion.27 = (bf16[2,1,1152,128]{2,3,1,0:T(8,128)(2,1)S(1)}, bf16[2,1,1152,128]{2,3,1,0:T(8,128)(2,1)S(1)}) fusion(f32[2,128]{1,0:T(2,128)S(1)} %get-tuple-element.45, f32[2,1152]{1,0:T(2,128)S(1)} %get-tuple-element.29, f32[2,128]{1,0:T(2,128)S(1)} %get-tuple-element.44, f32[2,1152]{1,0:T(2,128)S(1)} %get-tuple-element.28, f32[2]{0:T(128)S(1)} %get-tuple-element.51, ...), kind=kLoop, calls=%fused_computation.49 | loop fusion | flops 5013504 | bytes 2379800 | tf_op jit(solution)/shard_map/convert_element_type | solution.py:39
  24.0 3.3 %collective-permute-done = bf16[256,128]{1,0:T(8,128)(2,1)S(1)} collective-permute-done((bf16[256,128]{1,0:T(8,128)(2,1)S(1)}, bf16[256,128]{1,0:T(8,128)(2,1)S(1)}, u32[]{:S(2)}, u32[]{:S(2)}) %collective-permute-start) | collective-permute-done | bytes 65568 | tf_op jit(solution)/shard_map/ppermute | solution.py:16
  27.5 2.7 %collective-permute-start.2 = (bf16[256,384]{1,0:T(8,128)(2,1)S(1)}, bf16[256,384]{1,0:T(8,128)(2,1)S(1)}, u32[]{:S(2)}, u32[]{:S(2)}) collective-permute-start(bf16[256,384]{1,0:T(8,128)(2,1)S(1)} %constant_dynamic-update-slice_fusion), channel_id=1, source_target_pairs={{0,12},{4,16},{8,20},{12,24},{16,28},{20,32},{24,36},{28,40},{32,4... | collective-permute-start | bytes 589832 | tf_op jit(solution)/shard_map/ppermute | solution.py:16
  30.2 0.6 fusion.20
  30.8 0.8 %fusion.10 = f32[3,6,4096]{2,1,0:T(8,128)S(1)} fusion(s32[4096]{0:T(1024)S(1)} %pad_add_fusion, bf16[1,6,256]{2,1,0:T(8,128)(2,1)S(1)} %get-tuple-element.31, bf16[1,6,256]{2,1,0:T(8,128)(2,1)S(1)} %get-tuple-element.32, bf16[1,6,256]{2,1,0:T(8,128)(2,1)S(1)} %get-tuple-element.30), kind=kOutput, calls=%fused_computation.16 | convolution fusion | flops 38806528 | bytes 320512 | tf_op jit(solution)/shard_map/pc,kqc->kqp/dot_general | solution.py:78
  31.7 3.9 %convolution_bitcast_fusion = bf16[6,2,4096,128]{2,3,1,0:T(8,128)(2,1)S(1)} fusion(s32[4096]{0:T(1024)S(1)} %pad_add_fusion, bf16[6,2,128,256]{3,2,1,0:T(8,128)(2,1)S(1)} %get-tuple-element.49), kind=kOutput, calls=%fused_computation.6 | convolution fusion | flops 3222274048 | bytes 13385728 | tf_op jit(solution)/shard_map/pc,qrct->qrpt/dot_general | solution.py:60
  35.6 3.1 %fusion.2 = (f32[6,2048]{1,0:T(8,128)S(1)}, f32[6,2048]{1,0:T(8,128)S(1)}, f32[6,2048]{1,0:T(8,128)S(1)}, f32[6,2048]{1,0:T(8,128)S(1)}) fusion(bf16[6,2,4096,128]{2,3,1,0:T(8,128)(2,1)S(1)} %convolution_bitcast_fusion), kind=kLoop, calls=%fused_computation.9 | loop fusion | flops 18825216 | bytes 12779520 | tf_op jit(solution)/shard_map/qpt,qpt->qp/dot_general | solution.py:68
  38.9 0.6 fusion.39
  39.5 1.0 %fusion.8 = f32[3,2,4096]{2,1,0:T(2,128)S(1)} fusion(s32[4096]{0:T(1024)S(1)} %pad_add_fusion, bf16[3,2,256]{2,0,1:T(4,128)(2,1)S(1)} %pad_maximum_fusion.1), kind=kOutput, calls=%fused_computation.15 | convolution fusion | flops 13631488 | bytes 117760 | tf_op jit(solution)/shard_map/pc,kqc->kqp/dot_general | solution.py:78
  40.6 1.7 %convolution_bitcast_fusion.1 = bf16[2,2,4096,128]{2,3,1,0:T(8,128)(2,1)S(1)} fusion(s32[4096]{0:T(1024)S(1)} %pad_add_fusion, bf16[2,2,128,256]{3,2,1,0:T(8,128)(2,1)S(1)} %get-tuple-element.47), kind=kOutput, calls=%fused_computation.11 | convolution fusion | flops 1074790400 | bytes 4472832 | tf_op jit(solution)/shard_map/pc,qrct->qrpt/dot_general | solution.py:60
  42.3 1.0 %fusion.14 = (f32[2,2048]{1,0:T(2,128)S(1)}, f32[2,2048]{1,0:T(2,128)S(1)}, f32[2,2048]{1,0:T(2,128)S(1)}, f32[2,2048]{1,0:T(2,128)S(1)}) fusion(bf16[2,2,4096,128]{2,3,1,0:T(8,128)(2,1)S(1)} %convolution_bitcast_fusion.1), kind=kLoop, calls=%fused_computation.27 | loop fusion | flops 6275072 | bytes 4259840 | tf_op jit(solution)/shard_map/qpt,qpt->qp/dot_general | solution.py:68
  43.7 0.8 %copy.48 = f32[256,2,128]{2,1,0:T(2,128)} copy(f32[256,2,128]{0,2,1:T(8,128)S(1)} %bitcast.170) | data formatting | bytes 524288 | tf_op jit(solution)/shard_map/reshape | solution.py:126
  44.5 10.6 %all-to-all-start = ((f32[256,2,128]{2,1,0:T(2,128)}), f32[256,2,128]{2,1,0:T(2,128)S(1)}, u32[]{:S(2)}, u32[]{:S(2)}) async-start(f32[256,2,128]{2,1,0:T(2,128)} %copy.48), calls=%async_computation | async-start | bytes 524288 | tf_op jit(solution)/shard_map/all_to_all | solution.py:127
  55.2 0.6 dynamic_slice.3
  55.8 0.7 add_compare_fusion
  56.5 14.0 %all-to-all-done = f32[256,2,128]{2,1,0:T(2,128)S(1)} async-done(((f32[256,2,128]{2,1,0:T(2,128)}), f32[256,2,128]{2,1,0:T(2,128)S(1)}, u32[]{:S(2)}, u32[]{:S(2)}) %all-to-all-start) | async-done | bytes 262176 | tf_op jit(solution)/shard_map/all_to_all | solution.py:127
  71.2 0.7 select_bitcast_fusion
  72.0 0.6 copy.52
  (73 shorter events, 3.9 us)
Async XLA Ops:
  0.6 18.0 %copy-start = (s32[32]{0:T(128)S(1)}, s32[32]{0:T(128)}, u32[]{:S(2)}) copy-start(s32[32]{0:T(128)} %param.6) | copy-start | bytes 388
  0.6 19.9 %copy-start.1 = (s32[4,512]{1,0:T(4,128)S(1)}, s32[4,512]{1,0:T(4,128)}, u32[]{:S(2)}) copy-start(s32[4,512]{1,0:T(4,128)} %param.7) | copy-start | bytes 24580
  0.7 20.7 %copy-start.2 = (s32[4,512]{1,0:T(4,128)S(1)}, s32[4,512]{1,0:T(4,128)}, u32[]{:S(2)}) copy-start(s32[4,512]{1,0:T(4,128)} %param.8) | copy-start | bytes 24580
  9.7 17.6 %collective-permute-start.1 = (bf16[256,128]{1,0:T(8,128)(2,1)S(1)}, bf16[256,128]{1,0:T(8,128)(2,1)S(1)}, u32[]{:S(2)}, u32[]{:S(2)}) collective-permute-start(bf16[256,128]{1,0:T(8,128)(2,1)S(1)} %all_gather.3), channel_id=1, source_target_pairs={{0,252},{4,0},{8,4},{12,8},{16,12},{20,16},{24,20},{28,24},{32,28}... | collective-permute-start | bytes 196616 | tf_op jit(solution)/shard_map/ppermute | solution.py:16
  18.5 8.8 %collective-permute-start = (bf16[256,128]{1,0:T(8,128)(2,1)S(1)}, bf16[256,128]{1,0:T(8,128)(2,1)S(1)}, u32[]{:S(2)}, u32[]{:S(2)}) collective-permute-start(bf16[256,128]{1,0:T(8,128)(2,1)S(1)} %all_gather.3), channel_id=1, source_target_pairs={{0,4},{4,8},{8,12},{12,16},{16,20},{20,24},{24,28},{28,32},{32,36}... | collective-permute-start | bytes 196616 | tf_op jit(solution)/shard_map/ppermute | solution.py:16
  27.4 11.4 %collective-permute-start.3 = (bf16[256,384]{1,0:T(8,128)(2,1)S(1)}, bf16[256,384]{1,0:T(8,128)(2,1)S(1)}, u32[]{:S(2)}, u32[]{:S(2)}) collective-permute-start(bf16[256,384]{1,0:T(8,128)(2,1)S(1)} %constant_dynamic-update-slice_fusion), channel_id=1, source_target_pairs={{0,244},{4,248},{8,252},{12,0},{16,4},{20,8},{24,12},{28,16},{32,2... | collective-permute-start | bytes 589832 | tf_op jit(solution)/shard_map/ppermute | solution.py:16
  27.5 11.2 %collective-permute-start.2 = (bf16[256,384]{1,0:T(8,128)(2,1)S(1)}, bf16[256,384]{1,0:T(8,128)(2,1)S(1)}, u32[]{:S(2)}, u32[]{:S(2)}) collective-permute-start(bf16[256,384]{1,0:T(8,128)(2,1)S(1)} %constant_dynamic-update-slice_fusion), channel_id=1, source_target_pairs={{0,12},{4,16},{8,20},{12,24},{16,28},{20,32},{24,36},{28,40},{32,4... | collective-permute-start | bytes 589832 | tf_op jit(solution)/shard_map/ppermute | solution.py:16
  43.4 11.8 %copy-start.3 = (s32[4]{0:T(128)S(1)}, s32[4]{0:T(128)}, u32[]{:S(2)}) copy-start(s32[4]{0:T(128)} %param.9) | copy-start | bytes 52
  44.5 25.9 %all-to-all-start = ((f32[256,2,128]{2,1,0:T(2,128)}), f32[256,2,128]{2,1,0:T(2,128)S(1)}, u32[]{:S(2)}, u32[]{:S(2)}) async-start(f32[256,2,128]{2,1,0:T(2,128)} %copy.48), calls=%async_computation | async-start | bytes 524288 | tf_op jit(solution)/shard_map/all_to_all | solution.py:127
where the time goes:
time: 72.8 us; the launch traced here: 72.6 us
  starting transfers between devices  22.2 us (30%)
  waiting for transfers between devices  17.3 us (24%)
  other arithmetic  9.15 us (13%)
  matrix products  8.63 us (12%)
  blocking collectives  8.3 us (11%)
  local copies, waits for them, and re-layouts  5.9 us (8%)
  between operations  1.14 us (2%)
    all_to_all x1, waiting for transfers between devices, shards(): exchanged = lax.all_to_all(partial_value, ('tm', 'chan'), 0, 0, tiled=True)  14 us
    ppermute x4, starting transfers between devices, from_behind(): lax.ppermute(array, axis, [(i, (i + by) % peers) for i in range(peers)])  11.5 us
    all_to_all x1, starting transfers between devices, shards(): exchanged = lax.all_to_all(partial_value, ('tm', 'chan'), 0, 0, tiled=True)  10.6 us
    all_gather x1, blocking collectives, shards(): gathered = lax.all_gather(rounded, 'chan', axis=0, tiled=True)  8.3 us
    dot_general x2, matrix products, pair_sums(): jnp.einsum('pc,qrct->qrpt', pick, parts, preferred_element_type=jnp.bfloa...  5.6 us
    dot_general x2, other arithmetic, time_sum(): jnp.einsum('qpt,qpt->qp', left, right, preferred_element_type=jnp.float32)  4.04 us
    ppermute x4, waiting for transfers between devices, from_behind(): lax.ppermute(array, axis, [(i, (i + by) % peers) for i in range(peers)])  3.3 us
    dot_general x2, matrix products, pair_sums(): jnp.einsum('pc,kqc->kqp', pick, pieces, preferred_element_type=jnp.float32)  1.86 us
  transfers between devices with their start and end apart: 5, of which 2 were waited for; matrix products, arithmetic and copies ran while one was open for 21% of the time, Pallas kernels for 0%

commit v1 on v0

--- a/solution.py
+++ b/solution.py
@@ -90,7 +90,15 @@
     time_span = signal.shape[1]
     ntime = time_span * time_devices
     rounded = signal.astype(jnp.bfloat16)
-    gathered = lax.all_gather(rounded, "chan", axis=0, tiled=True)
+    gathered = jnp.concatenate(
+        lax.all_to_all(
+            jnp.stack([rounded for _ in range(lax.psum(1, axis_name="chan"))]),
+            axis_name="chan",
+            split_axis=0,
+            concat_axis=0,
+        ),
+        0,
+    )
     near = jnp.concatenate(
         [from_behind(gathered, "tm", 1), gathered, from_behind(gathered, "tm", -1)], axis=1
     )

time: 72.8 us -> 77.1 us (1.059)
  blocking collectives: 8.3 us -> 0 us
  starting transfers between devices: 22.2 us -> 28.5 us
  waiting for transfers between devices: 17.3 us -> 23 us
    all_gather x1 -> x0, blocking collectives: 8.3 us -> none  [shards(): gathered = lax.all_gather(rounded, 'chan', axis=0, tiled=True)]
    all_to_all x0 -> x1, starting transfers between devices: none -> 6.49 us  [shards(): lax.all_to_all(jnp.stack([rounded for _ in range(lax.psum(1, axis_name='c...]
    ppermute x4, waiting for transfers between devices: 3.3 us -> 8.84 us  [from_behind(): lax.ppermute(array, axis, [(i, (i + by) % peers) for i in range(peers)])]
    all_to_all x1, starting transfers between devices: 10.6 us -> 7.09 us  [shards(): exchanged = lax.all_to_all(partial_value, ('tm', 'chan'), 0, 0, tiled=True)]
    ppermute x4, starting transfers between devices: 11.5 us -> 14.9 us  [from_behind(): lax.ppermute(array, axis, [(i, (i + by) % peers) for i in range(peers)])]
  transfers between devices with their start and end apart: 5 -> 6, of which waited for: 2 -> 3; matrix products, arithmetic and copies ran while one was open for 21% -> 20% of each run, Pallas kernels for 0% -> 0%
where the time goes in v1:
time: 77.1 us; the launch traced here: 76.8 us
  starting transfers between devices  28.5 us (37%)
  waiting for transfers between devices  23 us (30%)
  other arithmetic  9.16 us (12%)
  matrix products  8.62 us (11%)
  local copies, waits for them, and re-layouts  6.49 us (8%)
  between operations  1.13 us (1%)
    ppermute x4, starting transfers between devices, from_behind(): lax.ppermute(array, axis, [(i, (i + by) % peers) for i in range(peers)])  14.9 us
    all_to_all x1, waiting for transfers between devices, shards(): exchanged = lax.all_to_all(partial_value, ('tm', 'chan'), 0, 0, tiled=True)  14.1 us
    ppermute x4, waiting for transfers between devices, from_behind(): lax.ppermute(array, axis, [(i, (i + by) % peers) for i in range(peers)])  8.84 us
    all_to_all x1, starting transfers between devices, shards(): exchanged = lax.all_to_all(partial_value, ('tm', 'chan'), 0, 0, tiled=True)  7.09 us
    all_to_all x1, starting transfers between devices, shards(): lax.all_to_all(jnp.stack([rounded for _ in range(lax.psum(1, axis_name='c...  6.49 us
    dot_general x2, matrix products, pair_sums(): jnp.einsum('pc,qrct->qrpt', pick, parts, preferred_element_type=jnp.bfloa...  5.59 us
    dot_general x2, other arithmetic, time_sum(): jnp.einsum('qpt,qpt->qp', left, right, preferred_element_type=jnp.float32)  4.04 us
    dot_general x2, matrix products, pair_sums(): jnp.einsum('pc,kqc->kqp', pick, pieces, preferred_element_type=jnp.float32)  1.86 us
  transfers between devices with their start and end apart: 6, of which 3 were waited for; matrix products, arithmetic and copies ran while one was open for 20% of the time, Pallas kernels for 0%

profile of v1, /device:TPU:1, one launch (start us, length us, event | category | flops | bytes accessed | tf_op | source)
XLA Modules:
  0.0 76.8 jit_solution(15301509758227744940)
XLA Ops:
  0.6 0.8 convert_element_type.133
  1.4 0.6 stack.89
  2.0 6.5 %all-to-all-start = ((bf16[4,64,128]{2,1,0:T(8,128)(2,1)}), bf16[4,64,128]{2,1,0:T(8,128)(2,1)S(1)}, u32[]{:S(2)}, u32[]{:S(2)}) async-start(bf16[4,64,128]{2,1,0:T(8,128)(2,1)} %stack.89), calls=%async_computation | async-start | bytes 131072 | tf_op jit(solution)/shard_map/all_to_all | solution.py:94
  8.7 0.6 gather_fusion.1
  9.3 0.6 gather_fusion
  10.7 1.0 %fusion.27 = (bf16[2,1,1152,128]{2,3,1,0:T(8,128)(2,1)S(1)}, bf16[2,1,1152,128]{2,3,1,0:T(8,128)(2,1)S(1)}) fusion(f32[2,128]{1,0:T(2,128)S(1)} %get-tuple-element.45, f32[2,1152]{1,0:T(2,128)S(1)} %get-tuple-element.29, f32[2,128]{1,0:T(2,128)S(1)} %get-tuple-element.44, f32[2,1152]{1,0:T(2,128)S(1)} %get-tuple-element.28, f32[2]{0:T(128)S(1)} %get-tuple-element.51, ...), kind=kLoop, calls=%fused_computation.49 | loop fusion | flops 5013504 | bytes 2379800 | tf_op jit(solution)/shard_map/convert_element_type | solution.py:39
  11.7 0.8 %fusion.25 = (bf16[6,1,384,128]{2,3,1,0:T(8,128)(2,1)S(1)}, bf16[6,1,384,128]{2,3,1,0:T(8,128)(2,1)S(1)}) fusion(f32[6,128]{1,0:T(8,128)S(1)} %get-tuple-element.43, f32[6,384]{1,0:T(8,128)S(1)} %get-tuple-element.36, f32[6,128]{1,0:T(8,128)S(1)} %get-tuple-element.42, f32[6,384]{1,0:T(8,128)S(1)} %get-tuple-element.35, f32[6]{0:T(128)S(1)} %get-tuple-element.55, ...), kind=kLoop, calls=%fused_computation.47 | loop fusion | flops 5013504 | bytes 1597512 | tf_op jit(solution)/shard_map/convert_element_type | solution.py:39
  14.1 8.8 %collective-permute-start.1 = (bf16[256,128]{1,0:T(8,128)(2,1)S(1)}, bf16[256,128]{1,0:T(8,128)(2,1)S(1)}, u32[]{:S(2)}, u32[]{:S(2)}) collective-permute-start(bf16[256,128]{1,0:T(8,128)(2,1)S(1)} %bitcast.172), channel_id=1, source_target_pairs={{0,252},{4,0},{8,4},{12,8},{16,12},{20,16},{24,20},{28,24},{32,28}... | collective-permute-start | bytes 196616 | tf_op jit(solution)/shard_map/ppermute | solution.py:16
  22.9 1.3 %collective-permute-done.1 = bf16[256,128]{1,0:T(8,128)(2,1)S(1)} collective-permute-done((bf16[256,128]{1,0:T(8,128)(2,1)S(1)}, bf16[256,128]{1,0:T(8,128)(2,1)S(1)}, u32[]{:S(2)}, u32[]{:S(2)}) %collective-permute-start.1) | collective-permute-done | bytes 65568 | tf_op jit(solution)/shard_map/ppermute | solution.py:16
  24.3 7.5 %collective-permute-done = bf16[256,128]{1,0:T(8,128)(2,1)S(1)} collective-permute-done((bf16[256,128]{1,0:T(8,128)(2,1)S(1)}, bf16[256,128]{1,0:T(8,128)(2,1)S(1)}, u32[]{:S(2)}, u32[]{:S(2)}) %collective-permute-start) | collective-permute-done | bytes 65568 | tf_op jit(solution)/shard_map/ppermute | solution.py:16
  31.9 6.0 %collective-permute-start.3 = (bf16[256,384]{1,0:T(8,128)(2,1)S(1)}, bf16[256,384]{1,0:T(8,128)(2,1)S(1)}, u32[]{:S(2)}, u32[]{:S(2)}) collective-permute-start(bf16[256,384]{1,0:T(8,128)(2,1)S(1)} %pad_maximum_fusion), channel_id=1, source_target_pairs={{0,244},{4,248},{8,252},{12,0},{16,4},{20,8},{24,12},{28,16},{32,2... | collective-permute-start | bytes 589832 | tf_op jit(solution)/shard_map/ppermute | solution.py:16
  37.9 0.6 fusion.20
  38.5 0.8 %fusion.10 = f32[3,6,4096]{2,1,0:T(8,128)S(1)} fusion(s32[4096]{0:T(1024)S(1)} %pad_add_fusion, bf16[1,6,256]{2,1,0:T(8,128)(2,1)S(1)} %get-tuple-element.31, bf16[1,6,256]{2,1,0:T(8,128)(2,1)S(1)} %get-tuple-element.32, bf16[1,6,256]{2,1,0:T(8,128)(2,1)S(1)} %get-tuple-element.30), kind=kOutput, calls=%fused_computation.16 | convolution fusion | flops 38806528 | bytes 320512 | tf_op jit(solution)/shard_map/pc,kqc->kqp/dot_general | solution.py:78
  39.4 3.9 %convolution_bitcast_fusion = bf16[6,2,4096,128]{2,3,1,0:T(8,128)(2,1)S(1)} fusion(s32[4096]{0:T(1024)S(1)} %pad_add_fusion, bf16[6,2,128,256]{3,2,1,0:T(8,128)(2,1)S(1)} %get-tuple-element.49), kind=kOutput, calls=%fused_computation.6 | convolution fusion | flops 3222274048 | bytes 13385728 | tf_op jit(solution)/shard_map/pc,qrct->qrpt/dot_general | solution.py:60
  43.3 3.1 %fusion.2 = (f32[6,2048]{1,0:T(8,128)S(1)}, f32[6,2048]{1,0:T(8,128)S(1)}, f32[6,2048]{1,0:T(8,128)S(1)}, f32[6,2048]{1,0:T(8,128)S(1)}) fusion(bf16[6,2,4096,128]{2,3,1,0:T(8,128)(2,1)S(1)} %convolution_bitcast_fusion), kind=kLoop, calls=%fused_computation.9 | loop fusion | flops 18825216 | bytes 12779520 | tf_op jit(solution)/shard_map/qpt,qpt->qp/dot_general | solution.py:68
  47.2 1.0 %fusion.8 = f32[3,2,4096]{2,1,0:T(2,128)S(1)} fusion(s32[4096]{0:T(1024)S(1)} %pad_add_fusion, bf16[3,2,256]{2,0,1:T(4,128)(2,1)S(1)} %pad_maximum_fusion.2), kind=kOutput, calls=%fused_computation.15 | convolution fusion | flops 13631488 | bytes 117760 | tf_op jit(solution)/shard_map/pc,kqc->kqp/dot_general | solution.py:78
  48.3 1.7 %convolution_bitcast_fusion.1 = bf16[2,2,4096,128]{2,3,1,0:T(8,128)(2,1)S(1)} fusion(s32[4096]{0:T(1024)S(1)} %pad_add_fusion, bf16[2,2,128,256]{3,2,1,0:T(8,128)(2,1)S(1)} %get-tuple-element.47), kind=kOutput, calls=%fused_computation.11 | convolution fusion | flops 1074790400 | bytes 4472832 | tf_op jit(solution)/shard_map/pc,qrct->qrpt/dot_general | solution.py:60
  50.0 1.0 %fusion.14 = (f32[2,2048]{1,0:T(2,128)S(1)}, f32[2,2048]{1,0:T(2,128)S(1)}, f32[2,2048]{1,0:T(2,128)S(1)}, f32[2,2048]{1,0:T(2,128)S(1)}) fusion(bf16[2,2,4096,128]{2,3,1,0:T(8,128)(2,1)S(1)} %convolution_bitcast_fusion.1), kind=kLoop, calls=%fused_computation.27 | loop fusion | flops 6275072 | bytes 4259840 | tf_op jit(solution)/shard_map/qpt,qpt->qp/dot_general | solution.py:68
  51.4 0.8 %copy.48 = f32[256,2,128]{2,1,0:T(2,128)} copy(f32[256,2,128]{0,2,1:T(8,128)S(1)} %bitcast.171) | data formatting | bytes 524288 | tf_op jit(solution)/shard_map/reshape | solution.py:134
  52.2 7.1 %all-to-all-start.1 = ((f32[256,2,128]{2,1,0:T(2,128)}), f32[256,2,128]{2,1,0:T(2,128)S(1)}, u32[]{:S(2)}, u32[]{:S(2)}) async-start(f32[256,2,128]{2,1,0:T(2,128)} %copy.48), calls=%async_computation.1 | async-start | bytes 524288 | tf_op jit(solution)/shard_map/all_to_all | solution.py:135
  59.9 0.7 add_compare_fusion
  60.6 14.1 %all-to-all-done.1 = f32[256,2,128]{2,1,0:T(2,128)S(1)} async-done(((f32[256,2,128]{2,1,0:T(2,128)}), f32[256,2,128]{2,1,0:T(2,128)S(1)}, u32[]{:S(2)}, u32[]{:S(2)}) %all-to-all-start.1) | async-done | bytes 262176 | tf_op jit(solution)/shard_map/all_to_all | solution.py:135
  75.5 0.7 select_bitcast_fusion
  76.2 0.6 copy.52
  (73 shorter events, 5.1 us)
Async XLA Ops:
  0.6 8.0 %copy-start = (s32[32]{0:T(128)S(1)}, s32[32]{0:T(128)}, u32[]{:S(2)}) copy-start(s32[32]{0:T(128)} %param.6) | copy-start | bytes 388
  2.0 12.0 %all-to-all-start = ((bf16[4,64,128]{2,1,0:T(8,128)(2,1)}), bf16[4,64,128]{2,1,0:T(8,128)(2,1)S(1)}, u32[]{:S(2)}, u32[]{:S(2)}) async-start(bf16[4,64,128]{2,1,0:T(8,128)(2,1)} %stack.89), calls=%async_computation | async-start | bytes 131072 | tf_op jit(solution)/shard_map/all_to_all | solution.py:94
  11.7 0.8 %copy-start.1 = (s32[4,512]{1,0:T(4,128)S(1)}, s32[4,512]{1,0:T(4,128)}, u32[]{:S(2)}) copy-start(s32[4,512]{1,0:T(4,128)} %param.7) | copy-start | bytes 24580
  11.7 1.6 %copy-start.2 = (s32[4,512]{1,0:T(4,128)S(1)}, s32[4,512]{1,0:T(4,128)}, u32[]{:S(2)}) copy-start(s32[4,512]{1,0:T(4,128)} %param.8) | copy-start | bytes 24580
  14.1 10.2 %collective-permute-start.1 = (bf16[256,128]{1,0:T(8,128)(2,1)S(1)}, bf16[256,128]{1,0:T(8,128)(2,1)S(1)}, u32[]{:S(2)}, u32[]{:S(2)}) collective-permute-start(bf16[256,128]{1,0:T(8,128)(2,1)S(1)} %bitcast.172), channel_id=1, source_target_pairs={{0,252},{4,0},{8,4},{12,8},{16,12},{20,16},{24,20},{28,24},{32,28}... | collective-permute-start | bytes 196616 | tf_op jit(solution)/shard_map/ppermute | solution.py:16
  22.9 8.8 %collective-permute-start = (bf16[256,128]{1,0:T(8,128)(2,1)S(1)}, bf16[256,128]{1,0:T(8,128)(2,1)S(1)}, u32[]{:S(2)}, u32[]{:S(2)}) collective-permute-start(bf16[256,128]{1,0:T(8,128)(2,1)S(1)} %bitcast.173), channel_id=1, source_target_pairs={{0,4},{4,8},{8,12},{12,16},{16,20},{20,24},{24,28},{28,32},{32,36}... | collective-permute-start | bytes 196616 | tf_op jit(solution)/shard_map/ppermute | solution.py:16
  31.8 14.6 %collective-permute-start.2 = (bf16[256,384]{1,0:T(8,128)(2,1)S(1)}, bf16[256,384]{1,0:T(8,128)(2,1)S(1)}, u32[]{:S(2)}, u32[]{:S(2)}) collective-permute-start(bf16[256,384]{1,0:T(8,128)(2,1)S(1)} %pad_maximum_fusion), channel_id=1, source_target_pairs={{0,12},{4,16},{8,20},{12,24},{16,28},{20,32},{24,36},{28,40},{32,4... | collective-permute-start | bytes 589832 | tf_op jit(solution)/shard_map/ppermute | solution.py:16
  31.9 14.6 %collective-permute-start.3 = (bf16[256,384]{1,0:T(8,128)(2,1)S(1)}, bf16[256,384]{1,0:T(8,128)(2,1)S(1)}, u32[]{:S(2)}, u32[]{:S(2)}) collective-permute-start(bf16[256,384]{1,0:T(8,128)(2,1)S(1)} %pad_maximum_fusion), channel_id=1, source_target_pairs={{0,244},{4,248},{8,252},{12,0},{16,4},{20,8},{24,12},{28,16},{32,2... | collective-permute-start | bytes 589832 | tf_op jit(solution)/shard_map/ppermute | solution.py:16
  51.1 8.3 %copy-start.3 = (s32[4]{0:T(128)S(1)}, s32[4]{0:T(128)}, u32[]{:S(2)}) copy-start(s32[4]{0:T(128)} %param.9) | copy-start | bytes 52
  52.2 22.5 %all-to-all-start.1 = ((f32[256,2,128]{2,1,0:T(2,128)}), f32[256,2,128]{2,1,0:T(2,128)S(1)}, u32[]{:S(2)}, u32[]{:S(2)}) async-start(f32[256,2,128]{2,1,0:T(2,128)} %copy.48), calls=%async_computation.1 | async-start | bytes 524288 | tf_op jit(solution)/shard_map/all_to_all | solution.py:135
